TPU v7x, 256 devices: a whole 4x4x8 slice. The times are simulated.
256 devices in a mesh: leaf: 2 (over core), row: 8 (over z), col: 16 (over y, x).
Axes of the slice: x: 4, y: 4, z: 8, core: 2. Of those that a mesh axis runs over, the one named last changes fastest.
Arguments:
- front: float32 [2, 8, 8, 128, 4, 16, 128], P('leaf', None, 'row', None, None, 'col'), as said below
- parent: float32 [4, 2, 8, 128, 4, 16, 128], P(None, 'leaf', 'row', None, None, 'col'), may hold values from -0.2 to 0.2
- tile_map: int32 [2, 56], replicated, may hold values from 0 to 63, as said below
- col_shift: int32 [4], replicated, may hold values from 0 to 7
Outputs:
- factored: float32 [2, 8, 8, 128, 4, 16, 128], P('leaf', None, 'row', None, None, 'col')
- new_parent: float32 [4, 2, 8, 128, 4, 16, 128], P(None, 'leaf', 'row', None, None, 'col')
Inputs may be any that keep to these rules, and one draw needn't show every extreme that they name: For each leaf the 8192 x 8192 matrix read from front is symmetric positive definite. Entry [l, e] names the parent tile joined by tile 8 + e of child l; no row repeats a value. The parent tile q = tile_map[l, e] has (q mod 16 + col_shift[q // 16]) mod 16 equal to (8 + e) mod 16. Among the tiles of one child whose indices are equal mod 8, at most 1 have parent tiles equal mod 16.
All inputs are finite; a program needn't handle non-finite values.
Results may differ from a plain program's by a relative error of at most 0.0001.
Values sent between devices are 32-bit elements; how exact they have to be, the bound alone decides.
No kernel may reach another device: no remote copies, remote signals or barrier semaphores. Data moves between devices by JAX's collectives and lax.ppermute only.
A program may use at most 128 MiB of HBM per device.

v0:
```python
import jax
import jax.numpy as jnp
from jax import lax
from jax.sharding import PartitionSpec as P

TILE = 128
PB = 512
PANELS = 2
NPIV = 1024
HIGHEST = lax.Precision.HIGHEST


def spread(value, axis, source):
    kept = jnp.where(lax.axis_index(axis) == source, value, 0).astype(value.dtype)
    return lax.psum(kept, axis)


def update_slots(working, next_rows, column_factor, slot_low, slot_high):
    product = jnp.einsum(
        "atp,bsp->atbs",
        next_rows,
        column_factor,
        precision=HIGHEST,
        preferred_element_type=jnp.float32,
    )
    return working.at[:, :, slot_low:slot_high, :].add(-product)


def per_device(front, parent, tile_map, col_shift):
    leaf_count = lax.axis_size("leaf")
    row_count = lax.axis_size("row")
    col_count = lax.axis_size("col")
    leaf_index = lax.axis_index("leaf")
    row_index = lax.axis_index("row")
    col_index = lax.axis_index("col")
    local_front = front[0, :, 0, :, :, 0, :]
    row_slots = local_front.shape[0]
    col_slots = local_front.shape[2]
    pivot_tiles = NPIV // TILE
    assert pivot_tiles == row_count and pivot_tiles <= col_count
    row_tiles = jnp.arange(row_slots, dtype=jnp.int32) * row_count + row_index
    col_tiles = jnp.arange(col_slots, dtype=jnp.int32) * col_count + col_index
    working = local_front
    top_rows = lax.all_gather(working[0], "row", axis=0, tiled=False)
    column_panel = top_rows.transpose(2, 3, 0, 1).reshape(col_slots, TILE, NPIV)
    first_cols = lax.all_gather(working[:, :, 0, :], "col", axis=0, tiled=False)
    row_panel = first_cols[:pivot_tiles].transpose(1, 2, 0, 3).reshape(row_slots, TILE, NPIV)
    diagonal_block = lax.all_gather(row_panel[0], "row", axis=0, tiled=True)
    lower_factor = jnp.linalg.cholesky(diagonal_block)
    stacked = jnp.concatenate(
        [row_panel[1:].reshape(-1, NPIV), column_panel.reshape(-1, NPIV)], axis=0
    )
    solved = lax.linalg.triangular_solve(
        lower_factor, stacked, left_side=False, lower=True, transpose_a=True
    )
    trailing_rows = (row_slots - 1) * TILE
    row_factor = solved[:trailing_rows].reshape(row_slots - 1, TILE, NPIV)
    column_factor = solved[trailing_rows:].reshape(col_slots, TILE, NPIV)
    column_factor = jnp.where((col_tiles >= pivot_tiles)[:, None, None], column_factor, 0.0)
    product = jnp.einsum(
        "atk,bsk->atbs",
        row_factor,
        column_factor,
        precision=HIGHEST,
        preferred_element_type=jnp.float32,
    )
    trailing = working[1:] - product
    own_col = jnp.minimum(col_index, pivot_tiles - 1)
    row_factor_cols = lax.dynamic_slice_in_dim(row_factor, own_col * TILE, TILE, 2)
    is_factor_col = (col_tiles < pivot_tiles)[None, None, :, None]
    trailing = jnp.where(is_factor_col, row_factor_cols[:, :, None, :], trailing)
    diag_rows = lax.dynamic_slice_in_dim(lower_factor, row_index * TILE, TILE, 0)
    diag_tile = lax.dynamic_slice_in_dim(diag_rows, own_col * TILE, TILE, 1)
    local_ids = jnp.arange(TILE, dtype=jnp.int32)
    global_row = row_index * TILE + local_ids[:, None]
    global_col = own_col * TILE + local_ids[None, :]
    diag_tile = jnp.where(global_row >= global_col, diag_tile, 0.0)
    top = jnp.where(is_factor_col[0], diag_tile[:, None, :], 0.0)
    top = jnp.broadcast_to(top, working[0].shape)
    working = jnp.concatenate([top[None], trailing], axis=0)
    factored = working.reshape(front.shape)
    contribution = jnp.where((col_tiles >= pivot_tiles)[None, None, :, None], working, 0.0)
    contrib_count = tile_map.shape[1]
    entry_ids = jnp.arange(contrib_count, dtype=jnp.int32)
    own_map = lax.dynamic_index_in_dim(tile_map, leaf_index, 0, keepdims=False)
    row_match = (row_tiles - pivot_tiles)[:, None] == entry_ids[None, :]
    row_targets = jnp.sum(jnp.where(row_match, own_map[None, :], 0), axis=1)
    row_valid = row_tiles >= pivot_tiles
    owner_count = leaf_count * row_count
    destination = row_targets % owner_count
    parent_row_slot = row_targets // owner_count
    slot_ids = jnp.arange(row_slots, dtype=jnp.int32)
    same_before = (
        (destination[None, :] == destination[:, None])
        & row_valid[None, :]
        & (slot_ids[None, :] < slot_ids[:, None])
    )
    rank_in_dest = jnp.sum(same_before.astype(jnp.int32), axis=1)
    capacity = (col_slots + row_count - 1) // row_count
    owner_ids = jnp.arange(owner_count, dtype=jnp.int32)
    capacity_ids = jnp.arange(capacity, dtype=jnp.int32)
    selection = (
        row_valid[None, None, :]
        & (destination[None, None, :] == owner_ids[:, None, None])
        & (rank_in_dest[None, None, :] == capacity_ids[None, :, None])
    )
    flattened = contribution.reshape(row_slots, -1)
    send_buffer = jnp.einsum(
        "oka,ax->okx",
        selection.astype(jnp.float32),
        flattened,
        precision=HIGHEST,
        preferred_element_type=jnp.float32,
    )
    chosen_slot = jnp.sum(jnp.where(selection, parent_row_slot[None, None, :], 0), axis=2)
    send_slots = jnp.where(jnp.any(selection, axis=2), chosen_slot, -1)
    received, received_slots = (
        lax.all_to_all(send_buffer, ("leaf", "row"), split_axis=0, concat_axis=0, tiled=True),
        lax.all_to_all(send_slots, ("leaf", "row"), split_axis=0, concat_axis=0, tiled=True),
    )
    received = received.reshape(leaf_count, row_count, capacity, -1)
    received_slots = received_slots.reshape(leaf_count, row_count, capacity)
    parent_local = parent[:, 0, 0, :, :, 0, :]
    parent_rows = parent_local.shape[0]
    parent_cols = parent_local.shape[2]
    row_place = (
        received_slots[None] == jnp.arange(parent_rows, dtype=jnp.int32)[:, None, None, None]
    ).astype(jnp.float32)
    by_leaf = jnp.einsum(
        "slrk,lrkx->slx", row_place, received, precision=HIGHEST, preferred_element_type=jnp.float32
    )
    by_leaf = by_leaf.reshape(parent_rows, leaf_count, TILE, col_slots, TILE)
    col_match = (col_tiles - pivot_tiles)[:, None] == entry_ids[None, :]
    col_targets = jnp.sum(jnp.where(col_match[None], tile_map[:, None, :], 0), axis=2)
    col_valid = col_tiles >= pivot_tiles
    parent_slot_ids = jnp.arange(parent_cols, dtype=jnp.int32)
    col_place = (
        col_valid[None, None, :]
        & (col_targets[:, None, :] // col_count == parent_slot_ids[None, :, None])
    ).astype(jnp.float32)
    assembled = jnp.einsum(
        "sltbv,lub->stuv", by_leaf, col_place, precision=HIGHEST, preferred_element_type=jnp.float32
    )
    new_parent = (parent_local + assembled).reshape(parent.shape)
    return (factored, new_parent)


def solution(mesh):
    return jax.shard_map(
        per_device,
        mesh=mesh,
        in_specs=(
            P("leaf", None, "row", None, None, "col", None),
            P(None, "leaf", "row", None, None, "col", None),
            P(),
            P(),
        ),
        out_specs=(
            P("leaf", None, "row", None, None, "col", None),
            P(None, "leaf", "row", None, None, "col", None),
        ),
        check_vma=False,
    )
```

profile of v0, /device:TPU:1, one launch (start us, length us, event | category | flops | bytes accessed | tf_op | source)
XLA Modules:
  0.0 730.9 jit_solution(1884247141406783807)
XLA Ops:
  12.2 78.9 %all-gather.8.cloned.1.call-done = f32[128,128,1,128]{3,1,2,0:T(8,128)} async-done(((f32[8,128,1,128]{3,1,2,0:T(8,128)}), f32[128,128,1,128]{3,1,2,0:T(8,128)}) %all-gather.8.cloned.1.call-update) | async-done | bytes 8388624 | tf_op jit(solution)/shard_map/all_gather | solution.py:46
  93.2 2.4 copy.88
  99.9 7.7 %all-to-all-start.1 = ((s32[16,1,1]{2,1,0:T(1,128)}), s32[16,1,1]{2,1,0:T(1,128)S(1)}, u32[]{:S(2)}, u32[]{:S(2)}) async-start(s32[16,1,1]{2,1,0:T(1,128)} %copy.67), calls=%async_computation.1 | async-start | bytes 16384 | tf_op jit(solution)/shard_map/all_to_all | solution.py:119
  107.8 22.4 %all-gather.10.cloned.1.call-done = f32[8,1,1,128,4,1,128]{6,3,5,4,2,1,0:T(8,128)} async-done(((f32[1,1,1,128,4,1,128]{6,3,5,4,2,1,0:T(8,128)}), f32[8,1,1,128,4,1,128]{6,3,5,4,2,1,0:T(8,128)}) %all-gather.10.cloned.1.call-update) | async-done | bytes 2097168 | tf_op jit(solution)/shard_map/all_gather | solution.py:44
  134.5 2.7 bitcast_dynamic-update-slice_fusion.1
  139.0 55.7 %all-gather.6.cloned.1.call-done = f32[1024,1024]{0,1:T(8,128)} async-done(((f32[128,1024]{0,1:T(8,128)}), f32[1024,1024]{0,1:T(8,128)}) %all-gather.6.cloned.1.call-update) | async-done | bytes 4194320 | tf_op jit(solution)/shard_map/all_gather | solution.py:48
  194.6 5.5 copy.59
  200.2 4.4 fusion.2
  206.6 11.7 %cholesky.223 = f32[128,128]{1,0:T(8,128)S(1)} custom-call(f32[128,128]{1,0:T(8,128)S(1)} %cholesky.580), custom_call_target="Cholesky" | custom-call | tf_op jit(solution)/shard_map/jit(cholesky)/cholesky | solution.py:49
  218.4 9.8 %custom-call.62 = f32[1,128,128]{1,2,0:T(8,128)S(1)} custom-call(f32[1,128,128]{2,1,0:T(8,128)S(1)} %get-tuple-element.80), custom_call_target="InvertDiagBlocksLowerTriangular" | custom-call | tf_op jit(solution)/shard_map/jit(cholesky)/cholesky | solution.py:49
  228.2 2.5 cholesky.255
  230.7 2.4 constant_dynamic-update-slice_fusion.30
  234.6 11.9 %cholesky.244 = f32[128,128]{1,0:T(8,128)S(1)} custom-call(f32[128,128]{1,0:T(8,128)S(1)} %cholesky.584), custom_call_target="Cholesky" | custom-call | tf_op jit(solution)/shard_map/jit(cholesky)/cholesky | solution.py:49
  247.2 9.8 %custom-call.63 = f32[1,128,128]{1,2,0:T(8,128)S(1)} custom-call(f32[1,128,128]{2,1,0:T(8,128)S(1)} %get-tuple-element.77), custom_call_target="InvertDiagBlocksLowerTriangular" | custom-call | tf_op jit(solution)/shard_map/jit(cholesky)/cholesky | solution.py:49
  260.3 11.7 %cholesky.468 = f32[128,128]{1,0:T(8,128)S(1)} custom-call(f32[128,128]{1,0:T(8,128)S(1)} %cholesky.589), custom_call_target="Cholesky" | custom-call | tf_op jit(solution)/shard_map/jit(cholesky)/cholesky | solution.py:49
  273.3 9.8 %custom-call.64 = f32[1,128,128]{1,2,0:T(8,128)S(1)} custom-call(f32[1,128,128]{2,1,0:T(8,128)S(1)} %get-tuple-element.74), custom_call_target="InvertDiagBlocksLowerTriangular" | custom-call | tf_op jit(solution)/shard_map/jit(cholesky)/cholesky | solution.py:49
  284.3 2.3 convolution_subtract_fusion.8
  286.7 12.1 %cholesky.487 = f32[128,128]{1,0:T(8,128)S(1)} custom-call(f32[128,128]{1,0:T(8,128)S(1)} %cholesky.594), custom_call_target="Cholesky" | custom-call | tf_op jit(solution)/shard_map/jit(cholesky)/cholesky | solution.py:49
  300.0 9.8 %custom-call.65 = f32[1,128,128]{1,2,0:T(8,128)S(1)} custom-call(f32[1,128,128]{2,1,0:T(8,128)S(1)} %get-tuple-element.71), custom_call_target="InvertDiagBlocksLowerTriangular" | custom-call | tf_op jit(solution)/shard_map/jit(cholesky)/cholesky | solution.py:49
  313.3 11.7 %cholesky.506 = f32[128,128]{1,0:T(8,128)S(1)} custom-call(f32[128,128]{1,0:T(8,128)S(1)} %cholesky.599), custom_call_target="Cholesky" | custom-call | tf_op jit(solution)/shard_map/jit(cholesky)/cholesky | solution.py:49
  326.4 9.9 %custom-call.66 = f32[1,128,128]{1,2,0:T(8,128)S(1)} custom-call(f32[1,128,128]{2,1,0:T(8,128)S(1)} %get-tuple-element.68), custom_call_target="InvertDiagBlocksLowerTriangular" | custom-call | tf_op jit(solution)/shard_map/jit(cholesky)/cholesky | solution.py:49
  339.6 11.7 %cholesky.526 = f32[128,128]{1,0:T(8,128)S(1)} custom-call(f32[128,128]{1,0:T(8,128)S(1)} %cholesky.604), custom_call_target="Cholesky" | custom-call | tf_op jit(solution)/shard_map/jit(cholesky)/cholesky | solution.py:49
  352.6 9.8 %custom-call.67 = f32[1,128,128]{1,2,0:T(8,128)S(1)} custom-call(f32[1,128,128]{2,1,0:T(8,128)S(1)} %get-tuple-element.65), custom_call_target="InvertDiagBlocksLowerTriangular" | custom-call | tf_op jit(solution)/shard_map/jit(cholesky)/cholesky | solution.py:49
  365.4 11.9 %cholesky.546 = f32[128,128]{1,0:T(8,128)S(1)} custom-call(f32[128,128]{1,0:T(8,128)S(1)} %cholesky.609), custom_call_target="Cholesky" | custom-call | tf_op jit(solution)/shard_map/jit(cholesky)/cholesky | solution.py:49
  378.7 9.8 %custom-call.68 = f32[1,128,128]{1,2,0:T(8,128)S(1)} custom-call(f32[1,128,128]{2,1,0:T(8,128)S(1)} %get-tuple-element.62), custom_call_target="InvertDiagBlocksLowerTriangular" | custom-call | tf_op jit(solution)/shard_map/jit(cholesky)/cholesky | solution.py:49
  391.1 11.7 %cholesky.564 = f32[128,128]{1,0:T(8,128)S(1)} custom-call(f32[128,128]{1,0:T(8,128)S(1)} %convolution_subtract_fusion.12), custom_call_target="Cholesky" | custom-call | tf_op jit(solution)/shard_map/jit(cholesky)/cholesky | solution.py:49
  409.7 6.7 fusion.3
  416.4 23.3 %while.1 = (s32[]{:T(128)}, f32[1024,1024]{1,0:T(8,128)}, s32[8,2]{0,1:T(2,128)S(1)}, f32[8,128,128]{2,1,0:T(8,128)S(1)}, s32[]{:T(128)}) while((s32[]{:T(128)}, f32[1024,1024]{1,0:T(8,128)}, s32[8,2]{0,1:T(2,128)S(1)}, f32[8,128,128]{2,1,0:T(8,128)S(1)}, s32[]{:T(128)}) %tuple.72), condition=%wide.while_cond, body=%wide.while_body.sunk | while | flops 2 | bytes 131189 | solution.py:53
  439.7 79.0 %custom-call.69 = f32[8,128,128]{1,2,0:T(8,128)S(1)} custom-call(f32[8,128,128]{2,1,0:T(8,128)S(1)} %get-tuple-element.9), custom_call_target="InvertDiagBlocksLowerTriangular" | custom-call | tf_op jit(solution)/shard_map/triangular_solve | solution.py:53
  520.8 2.5 convolution_subtract_fusion.3
  524.2 3.7 convolution_subtract_fusion.5
  528.9 4.9 convolution_subtract_fusion.2
  534.9 6.2 fusion.12
  542.0 7.3 %convolution_subtract_fusion.1 = f32[1408,128]{1,0:T(8,128)S(1)} fusion(f32[1408,640]{0,1:T(8,128)S(1)} %get-tuple-element.42, f32[1408,1024]{1,0:T(8,128)} %bitcast_dynamic-update-slice_fusion.2, f32[1024,1024]{1,0:T(8,128)} %get-tuple-element.146), kind=kOutput, calls=%fused_computation.23 | convolution fusion | flops 1384300544 | bytes 5373952 | tf_op jit(solution)/shard_map/triangular_solve | solution.py:53
  550.2 8.6 %convolution_subtract_fusion = f32[1408,128]{1,0:T(8,128)S(1)} fusion(f32[1408,768]{0,1:T(8,128)S(1)} %get-tuple-element.38, f32[1408,1024]{1,0:T(8,128)} %bitcast_dynamic-update-slice_fusion.2, f32[1024,1024]{1,0:T(8,128)} %get-tuple-element.146), kind=kOutput, calls=%fused_computation.22 | convolution fusion | flops 1661124608 | bytes 6160384 | tf_op jit(solution)/shard_map/triangular_solve | solution.py:53
  559.7 10.1 %convolution_subtract_fusion.4 = f32[1408,128]{1,0:T(8,128)S(1)} fusion(f32[1408,896]{0,1:T(8,128)S(1)} %get-tuple-element.34, f32[1408,1024]{1,0:T(8,128)} %bitcast_dynamic-update-slice_fusion.2, f32[1024,1024]{1,0:T(8,128)} %get-tuple-element.146), kind=kOutput, calls=%fused_computation.26 | convolution fusion | flops 1937948672 | bytes 6946816 | tf_op jit(solution)/shard_map/triangular_solve | solution.py:53
  573.1 5.1 copy.62
  582.2 9.0 %fusion.23 = f32[7,128,4,128]{3,1,2,0:T(8,128)S(1)} fusion(f32[1,8,1,128,4,1,128]{6,3,4,1,5,2,0:T(8,128)} %copy-done.2, f32[7,128,1024,1]{2,1,3,0:T(8,128)} %bitcast.180, f32[4,128,1024,1]{2,1,0,3:T(8,128)} %bitcast.183, f32[7,128,128]{2,1,0:T(8,128)S(1)} %constant_dynamic-slice_fusion.2, pred[4]{0:T(512)(128)(4,1)S(1)} %get-tuple-element.92), kind=kOutput, calls=%fused_computation.42 | convolution fusion | flops 5638062080 | bytes 9895940 | tf_op jit(solution)/shard_map/atk,bsk->atbs/dot_general | solution.py:60
  591.2 2.4 copy.65
  593.6 3.7 concatenate.33
  597.4 3.8 convolution_bitcast_fusion
  601.2 6.3 copy.66
  607.5 10.2 %all-to-all-start = ((f32[16,1,65536]{2,1,0:T(1,128)}), f32[16,1,65536]{2,1,0:T(1,128)}, u32[]{:S(2)}, u32[]{:S(2)}) async-start(f32[16,1,65536]{2,1,0:T(1,128)} %copy.66), calls=%async_computation | async-start | bytes 8388608 | tf_op jit(solution)/shard_map/all_to_all | solution.py:118
  618.7 3.5 copy.69
  622.2 88.3 %all-to-all-done = f32[16,1,65536]{2,1,0:T(1,128)} async-done(((f32[16,1,65536]{2,1,0:T(1,128)}), f32[16,1,65536]{2,1,0:T(1,128)}, u32[]{:S(2)}, u32[]{:S(2)}) %all-to-all-start) | async-done | bytes 4194336 | tf_op jit(solution)/shard_map/all_to_all | solution.py:118
  710.5 7.8 %convolution_bitcast_fusion.1 = f32[4,2,65536]{2,0,1:T(4,128)} fusion(f32[16,1,65536]{2,1,0:T(1,128)} %all-to-all-done, s32[2,8]{1,0:T(2,128)S(1)} %eq.135), kind=kOutput, calls=%fused_computation.3 | convolution fusion | flops 50331712 | bytes 6291520 | tf_op jit(solution)/shard_map/slrk,lrkx->slx/dot_general | solution.py:129
  718.3 3.0 reshape.514
  721.3 2.8 fusion.27
  (127 shorter events, 86.5 us)
Async XLA Ops:
  7.2 4.2 slice-start.1
  7.2 83.8 %all-gather.8.cloned.1.call-start = ((), (), s32[]{:S(2)}) async-start(), calls=%async_computation.3 | async-start | bytes 8912896 | tf_op jit(solution)/shard_map/all_gather | solution.py:46
  9.1 1.3 copy-start.2
  11.3 118.9 %all-gather.10.cloned.1.call-start = ((), (), s32[]{:S(2)}) async-start(), calls=%async_computation.4 | async-start | bytes 2359296 | tf_op jit(solution)/shard_map/all_gather | solution.py:44
  12.1 182.5 %all-gather.6.cloned.1.call-start = ((), (), s32[]{:S(2)}) async-start(), calls=%async_computation.2 | async-start | bytes 4718592 | tf_op jit(solution)/shard_map/all_gather | solution.py:48
  91.0 2.2 slice-start
  93.2 5.4 copy-start.4
  95.6 1.9 copy-start
  99.9 507.6 %all-to-all-start.1 = ((s32[16,1,1]{2,1,0:T(1,128)}), s32[16,1,1]{2,1,0:T(1,128)S(1)}, u32[]{:S(2)}, u32[]{:S(2)}) async-start(s32[16,1,1]{2,1,0:T(1,128)} %copy.67), calls=%async_computation.1 | async-start | bytes 16384 | tf_op jit(solution)/shard_map/all_to_all | solution.py:119
  204.6 2.0 copy-start.1
  607.5 103.0 %all-to-all-start = ((f32[16,1,65536]{2,1,0:T(1,128)}), f32[16,1,65536]{2,1,0:T(1,128)}, u32[]{:S(2)}, u32[]{:S(2)}) async-start(f32[16,1,65536]{2,1,0:T(1,128)} %copy.66), calls=%async_computation | async-start | bytes 8388608 | tf_op jit(solution)/shard_map/all_to_all | solution.py:118
  622.2 99.2 %copy-start.3 = (f32[4,1,1,128,4,1,128]{6,5,4,3,2,1,0:T(1,128)S(1)}, f32[4,1,1,128,4,1,128]{6,5,4,3,2,1,0:T(1,128)}, u32[]{:S(2)}) copy-start(f32[4,1,1,128,4,1,128]{6,5,4,3,2,1,0:T(1,128)} %param.5) | copy-start | bytes 3145732
Sparse Core Ops, SparseCore 0:
  11.4 79.5 all-gather.7
  92.8 37.3 all-gather.9
  132.5 62.1 all-gather.5
where the time goes:
time: 737 us; the launch traced here: 731 us
  other arithmetic  266 us (36%)
  waiting for transfers between devices  245 us (33%)
  matrix products  98.3 us (13%)
  local copies, waits for them, and re-layouts  84.2 us (11%)
  between operations  19.4 us (3%)
  starting transfers between devices  18 us (2%)
    another operation x30, other arithmetic, per_device(): lower_factor = jnp.linalg.cholesky(diagonal_block)  172 us
    all_to_all x1, waiting for transfers between devices, per_device(): lax.all_to_all(send_buffer, ('leaf', 'row'), split_axis=0, concat_axis=0,...  88.3 us
    another operation x3, other arithmetic, per_device(): lax.linalg.triangular_solve(lower_factor, stacked, left_side=False, lower...  85.7 us
    all_gather x1, waiting for transfers between devices, per_device(): first_cols = lax.all_gather(working[:, :, 0, :], 'col', axis=0, tiled=False)  78.9 us
    all_gather x1, waiting for transfers between devices, per_device(): diagonal_block = lax.all_gather(row_panel[0], 'row', axis=0, tiled=True)  55.7 us
    another operation x15, matrix products, per_device(): lax.linalg.triangular_solve(lower_factor, stacked, left_side=False, lower...  51.9 us
    another operation x24, local copies, waits for them, and re-layouts  23.1 us
    another operation x14, matrix products, per_device(): lower_factor = jnp.linalg.cholesky(diagonal_block)  23.1 us
  transfers between devices with their start and end apart: 5, of which 4 were waited for; matrix products, arithmetic and copies ran while one was open for 58% of the time, Pallas kernels for 0%

commit v1 on v0

--- a/solution.py
+++ b/solution.py
@@ -45,7 +45,18 @@
     column_panel = top_rows.transpose(2, 3, 0, 1).reshape(col_slots, TILE, NPIV)
     first_cols = lax.all_gather(working[:, :, 0, :], "col", axis=0, tiled=False)
     row_panel = first_cols[:pivot_tiles].transpose(1, 2, 0, 3).reshape(row_slots, TILE, NPIV)
-    diagonal_block = lax.all_gather(row_panel[0], "row", axis=0, tiled=True)
+
+    def load_entries(body, named_axis):
+        buffers = []
+        nd = jax.lax.axis_size(named_axis)
+        for j0 in range(body.ndim):
+            buffers.append(nd if j0 == 0 else 1)
+        block_last = jax.lax.all_to_all(
+            jnp.tile(body, buffers), named_axis, split_axis=0, concat_axis=0, tiled=True
+        )
+        return block_last
+
+    diagonal_block = load_entries(row_panel[0], "row")
     lower_factor = jnp.linalg.cholesky(diagonal_block)
     stacked = jnp.concatenate(
         [row_panel[1:].reshape(-1, NPIV), column_panel.reshape(-1, NPIV)], axis=0

time: 737 us -> 771 us (1.046)
  waiting for transfers between devices: 245 us -> 271 us
    all_gather x1, waiting for transfers between devices: 22.4 us -> 85.5 us  [per_device(): top_rows = lax.all_gather(working[0], 'row', axis=0, tiled=False)]
    all_gather x1 -> x0, waiting for transfers between devices: 55.7 us -> none  [per_device(): diagonal_block = lax.all_gather(row_panel[0], 'row', axis=0, tiled=True)]
    all_to_all x0 -> x1, waiting for transfers between devices: none -> 17.6 us  [load_entries(): jax.lax.all_to_all(jnp.tile(body, buffers), named_axis, split_axis=0, con...]
    all_to_all x0 -> x2, local copies, waits for them, and re-layouts: none -> 10.2 us  [load_entries(): jax.lax.all_to_all(jnp.tile(body, buffers), named_axis, split_axis=0, con...]
    another operation x24 -> x25, local copies, waits for them, and re-layouts: 23.1 us -> 25.5 us
  transfers between devices with their start and end apart: 5 -> 5, of which waited for: 4 -> 4; matrix products, arithmetic and copies ran while one was open for 58% -> 56% of each run, Pallas kernels for 0% -> 0%
where the time goes in v1:
time: 771 us; the launch traced here: 765 us
  waiting for transfers between devices  271 us (35%)
  other arithmetic  265 us (34%)
  matrix products  98.5 us (13%)
  local copies, waits for them, and re-layouts  90.6 us (12%)
  between operations  21.1 us (3%)
  starting transfers between devices  18.3 us (2%)
    another operation x30, other arithmetic, per_device(): lower_factor = jnp.linalg.cholesky(diagonal_block)  172 us
    all_to_all x1, waiting for transfers between devices, per_device(): lax.all_to_all(send_buffer, ('leaf', 'row'), split_axis=0, concat_axis=0,...  88.1 us
    another operation x3, other arithmetic, per_device(): lax.linalg.triangular_solve(lower_factor, stacked, left_side=False, lower...  85.7 us
    all_gather x1, waiting for transfers between devices, per_device(): top_rows = lax.all_gather(working[0], 'row', axis=0, tiled=False)  85.5 us
    all_gather x1, waiting for transfers between devices, per_device(): first_cols = lax.all_gather(working[:, :, 0, :], 'col', axis=0, tiled=False)  79.7 us
    another operation x15, matrix products, per_device(): lax.linalg.triangular_solve(lower_factor, stacked, left_side=False, lower...  51.9 us
    another operation x14, matrix products, per_device(): lower_factor = jnp.linalg.cholesky(diagonal_block)  23.2 us
    another operation x24, local copies, waits for them, and re-layouts  23.1 us
  transfers between devices with their start and end apart: 5, of which 4 were waited for; matrix products, arithmetic and copies ran while one was open for 56% of the time, Pallas kernels for 0%

profile of v1, /device:TPU:1, one launch (start us, length us, event | category | flops | bytes accessed | tf_op | source)
XLA Modules:
  0.0 764.6 jit_solution(17324432708847414662)
XLA Ops:
  12.1 79.7 %all-gather.5.cloned.1.call-done = f32[128,128,1,128]{3,1,2,0:T(8,128)} async-done(((f32[8,128,1,128]{3,1,2,0:T(8,128)}), f32[128,128,1,128]{3,1,2,0:T(8,128)}) %all-gather.5.cloned.1.call-update) | async-done | bytes 8388624 | tf_op jit(solution)/shard_map/all_gather | solution.py:46
  91.8 2.5 slice.278
  98.8 6.9 all-to-all-start
  107.9 85.5 %all-gather.7.cloned.1.call-done = f32[8,1,1,128,4,1,128]{6,3,5,4,2,1,0:T(8,128)} async-done(((f32[1,1,1,128,4,1,128]{6,3,5,4,2,1,0:T(8,128)}), f32[8,1,1,128,4,1,128]{6,3,5,4,2,1,0:T(8,128)}) %all-gather.7.cloned.1.call-update) | async-done | bytes 2097168 | tf_op jit(solution)/shard_map/all_gather | solution.py:44
  195.4 2.5 slice.280
  200.0 2.7 bitcast_dynamic-update-slice_fusion.1
  204.4 17.6 %all-to-all-done = f32[8,128,1024]{1,2,0:T(8,128)} async-done(((f32[8,128,1024]{1,2,0:T(8,128)}), f32[8,128,1024]{1,2,0:T(8,128)}, u32[]{:S(2)}, u32[]{:S(2)}) %all-to-all-start) | async-done | bytes 4194336 | tf_op jit(solution)/shard_map/all_to_all | solution.py:54
  222.0 3.8 all-to-all-start.2
  225.9 4.7 copy_bitcast_fusion
  230.6 5.5 copy.74
  236.1 4.1 fusion.2
  242.2 11.7 %cholesky.223 = f32[128,128]{1,0:T(8,128)S(1)} custom-call(f32[128,128]{1,0:T(8,128)S(1)} %cholesky.580), custom_call_target="Cholesky" | custom-call | tf_op jit(solution)/shard_map/jit(cholesky)/cholesky | solution.py:60
  254.0 9.8 %custom-call.62 = f32[1,128,128]{1,2,0:T(8,128)S(1)} custom-call(f32[1,128,128]{2,1,0:T(8,128)S(1)} %get-tuple-element.82), custom_call_target="InvertDiagBlocksLowerTriangular" | custom-call | tf_op jit(solution)/shard_map/jit(cholesky)/cholesky | solution.py:60
  263.8 2.5 cholesky.255
  270.2 11.7 %cholesky.244 = f32[128,128]{1,0:T(8,128)S(1)} custom-call(f32[128,128]{1,0:T(8,128)S(1)} %cholesky.584), custom_call_target="Cholesky" | custom-call | tf_op jit(solution)/shard_map/jit(cholesky)/cholesky | solution.py:60
  282.6 10.0 %custom-call.63 = f32[1,128,128]{1,2,0:T(8,128)S(1)} custom-call(f32[1,128,128]{2,1,0:T(8,128)S(1)} %get-tuple-element.79), custom_call_target="InvertDiagBlocksLowerTriangular" | custom-call | tf_op jit(solution)/shard_map/jit(cholesky)/cholesky | solution.py:60
  295.9 11.7 %cholesky.468 = f32[128,128]{1,0:T(8,128)S(1)} custom-call(f32[128,128]{1,0:T(8,128)S(1)} %cholesky.589), custom_call_target="Cholesky" | custom-call | tf_op jit(solution)/shard_map/jit(cholesky)/cholesky | solution.py:60
  308.9 9.8 %custom-call.64 = f32[1,128,128]{1,2,0:T(8,128)S(1)} custom-call(f32[1,128,128]{2,1,0:T(8,128)S(1)} %get-tuple-element.76), custom_call_target="InvertDiagBlocksLowerTriangular" | custom-call | tf_op jit(solution)/shard_map/jit(cholesky)/cholesky | solution.py:60
  322.2 12.1 %cholesky.487 = f32[128,128]{1,0:T(8,128)S(1)} custom-call(f32[128,128]{1,0:T(8,128)S(1)} %cholesky.594), custom_call_target="Cholesky" | custom-call | tf_op jit(solution)/shard_map/jit(cholesky)/cholesky | solution.py:60
  335.6 9.8 %custom-call.65 = f32[1,128,128]{1,2,0:T(8,128)S(1)} custom-call(f32[1,128,128]{2,1,0:T(8,128)S(1)} %get-tuple-element.73), custom_call_target="InvertDiagBlocksLowerTriangular" | custom-call | tf_op jit(solution)/shard_map/jit(cholesky)/cholesky | solution.py:60
  348.9 11.7 %cholesky.506 = f32[128,128]{1,0:T(8,128)S(1)} custom-call(f32[128,128]{1,0:T(8,128)S(1)} %cholesky.599), custom_call_target="Cholesky" | custom-call | tf_op jit(solution)/shard_map/jit(cholesky)/cholesky | solution.py:60
  362.0 9.8 %custom-call.66 = f32[1,128,128]{1,2,0:T(8,128)S(1)} custom-call(f32[1,128,128]{2,1,0:T(8,128)S(1)} %get-tuple-element.70), custom_call_target="InvertDiagBlocksLowerTriangular" | custom-call | tf_op jit(solution)/shard_map/jit(cholesky)/cholesky | solution.py:60
  375.3 11.7 %cholesky.526 = f32[128,128]{1,0:T(8,128)S(1)} custom-call(f32[128,128]{1,0:T(8,128)S(1)} %cholesky.604), custom_call_target="Cholesky" | custom-call | tf_op jit(solution)/shard_map/jit(cholesky)/cholesky | solution.py:60
  388.2 9.8 %custom-call.67 = f32[1,128,128]{1,2,0:T(8,128)S(1)} custom-call(f32[1,128,128]{2,1,0:T(8,128)S(1)} %get-tuple-element.67), custom_call_target="InvertDiagBlocksLowerTriangular" | custom-call | tf_op jit(solution)/shard_map/jit(cholesky)/cholesky | solution.py:60
  401.0 11.7 %cholesky.546 = f32[128,128]{1,0:T(8,128)S(1)} custom-call(f32[128,128]{1,0:T(8,128)S(1)} %cholesky.609), custom_call_target="Cholesky" | custom-call | tf_op jit(solution)/shard_map/jit(cholesky)/cholesky | solution.py:60
  414.1 9.9 %custom-call.68 = f32[1,128,128]{1,2,0:T(8,128)S(1)} custom-call(f32[1,128,128]{2,1,0:T(8,128)S(1)} %get-tuple-element.64), custom_call_target="InvertDiagBlocksLowerTriangular" | custom-call | tf_op jit(solution)/shard_map/jit(cholesky)/cholesky | solution.py:60
  426.7 11.7 %cholesky.564 = f32[128,128]{1,0:T(8,128)S(1)} custom-call(f32[128,128]{1,0:T(8,128)S(1)} %convolution_subtract_fusion.12), custom_call_target="Cholesky" | custom-call | tf_op jit(solution)/shard_map/jit(cholesky)/cholesky | solution.py:60
  445.3 6.7 fusion.3
  452.0 23.3 %while.1 = (s32[]{:T(128)}, f32[1024,1024]{1,0:T(8,128)}, s32[8,2]{0,1:T(2,128)S(1)}, f32[8,128,128]{2,1,0:T(8,128)S(1)}, s32[]{:T(128)}) while((s32[]{:T(128)}, f32[1024,1024]{1,0:T(8,128)}, s32[8,2]{0,1:T(2,128)S(1)}, f32[8,128,128]{2,1,0:T(8,128)S(1)}, s32[]{:T(128)}) %tuple.73), condition=%wide.while_cond, body=%wide.while_body.sunk | while | flops 2 | bytes 131189 | solution.py:64
  475.3 79.0 %custom-call.69 = f32[8,128,128]{1,2,0:T(8,128)S(1)} custom-call(f32[8,128,128]{2,1,0:T(8,128)S(1)} %get-tuple-element.9), custom_call_target="InvertDiagBlocksLowerTriangular" | custom-call | tf_op jit(solution)/shard_map/triangular_solve | solution.py:64
  556.4 2.5 convolution_subtract_fusion.3
  559.8 3.7 convolution_subtract_fusion.5
  564.5 4.9 convolution_subtract_fusion.2
  570.5 6.2 fusion.12
  577.6 7.3 convolution_subtract_fusion.1
  585.8 8.6 %convolution_subtract_fusion = f32[1408,128]{1,0:T(8,128)S(1)} fusion(f32[1408,768]{0,1:T(8,128)S(1)} %get-tuple-element.40, f32[1408,1024]{1,0:T(8,128)} %bitcast_dynamic-update-slice_fusion.2, f32[1024,1024]{1,0:T(8,128)} %get-tuple-element.147), kind=kOutput, calls=%fused_computation.22 | convolution fusion | flops 1661124608 | bytes 6160384 | tf_op jit(solution)/shard_map/triangular_solve | solution.py:64
  595.3 10.1 %convolution_subtract_fusion.4 = f32[1408,128]{1,0:T(8,128)S(1)} fusion(f32[1408,896]{0,1:T(8,128)S(1)} %get-tuple-element.36, f32[1408,1024]{1,0:T(8,128)} %bitcast_dynamic-update-slice_fusion.2, f32[1024,1024]{1,0:T(8,128)} %get-tuple-element.147), kind=kOutput, calls=%fused_computation.26 | convolution fusion | flops 1937948672 | bytes 6946816 | tf_op jit(solution)/shard_map/triangular_solve | solution.py:64
  608.7 5.1 copy.78
  617.8 9.0 %fusion.23 = f32[7,128,4,128]{3,1,2,0:T(8,128)S(1)} fusion(f32[1,8,1,128,4,1,128]{6,3,4,1,5,2,0:T(8,128)} %copy-done.2, f32[7,128,1024,1]{2,1,3,0:T(8,128)} %bitcast.188, f32[4,128,1024,1]{2,1,0,3:T(8,128)} %bitcast.191, f32[7,128,128]{2,1,0:T(8,128)S(1)} %constant_dynamic-slice_fusion.2, pred[4]{0:T(512)(128)(4,1)S(1)} %get-tuple-element.94), kind=kOutput, calls=%fused_computation.42 | convolution fusion | flops 5638062080 | bytes 9895940 | tf_op jit(solution)/shard_map/atk,bsk->atbs/dot_general | solution.py:71
  629.2 3.7 concatenate.33
  633.0 3.8 convolution_bitcast_fusion
  636.8 6.3 copy.82
  643.1 7.6 all-to-all-start.1
  651.7 3.5 copy.85
  655.2 88.1 %all-to-all-done.1 = f32[16,1,65536]{2,1,0:T(1,128)} async-done(((f32[16,1,65536]{2,1,0:T(1,128)}), f32[16,1,65536]{2,1,0:T(1,128)}, u32[]{:S(2)}, u32[]{:S(2)}) %all-to-all-start.1) | async-done | bytes 4194336 | tf_op jit(solution)/shard_map/all_to_all | solution.py:129
  743.3 7.8 %convolution_bitcast_fusion.1 = f32[4,2,65536]{2,0,1:T(4,128)} fusion(f32[16,1,65536]{2,1,0:T(1,128)} %all-to-all-done.1, s32[2,8]{1,0:T(2,128)S(1)} %eq.135), kind=kOutput, calls=%fused_computation.3 | convolution fusion | flops 50331712 | bytes 6291520 | tf_op jit(solution)/shard_map/slrk,lrkx->slx/dot_general | solution.py:140
  751.1 3.0 reshape.521
  754.1 2.8 fusion.27
  (127 shorter events, 92.8 us)
Async XLA Ops:
  8.0 83.8 %all-gather.5.cloned.1.call-start = ((), (), s32[]{:S(2)}) async-start(), calls=%async_computation.3 | async-start | bytes 8912896 | tf_op jit(solution)/shard_map/all_gather | solution.py:46
  9.9 1.3 copy-start.2
  94.3 1.9 copy-start
  98.8 6.9 slice-start
  98.8 7.7 %copy-start.4 = (s32[2,56]{1,0:T(2,128)S(1)}, s32[2,56]{1,0:T(2,128)}, u32[]{:S(2)}) copy-start(s32[2,56]{1,0:T(2,128)} %param.6) | copy-start | bytes 1348
  98.8 123.3 %all-to-all-start = ((f32[8,128,1024]{1,2,0:T(8,128)}), f32[8,128,1024]{1,2,0:T(8,128)}, u32[]{:S(2)}, u32[]{:S(2)}) async-start(f32[8,128,1024]{1,2,0:T(8,128)} %tile.9), calls=%async_computation | async-start | bytes 8388608 | tf_op jit(solution)/shard_map/all_to_all | solution.py:54
  105.7 87.7 %all-gather.7.cloned.1.call-start = ((), (), s32[]{:S(2)}) async-start(), calls=%async_computation.4 | async-start | bytes 2359296 | tf_op jit(solution)/shard_map/all_gather | solution.py:44
  222.0 421.0 %all-to-all-start.2 = ((s32[16,1,1]{2,1,0:T(1,128)}), s32[16,1,1]{2,1,0:T(1,128)S(1)}, u32[]{:S(2)}, u32[]{:S(2)}) async-start(s32[16,1,1]{2,1,0:T(1,128)} %copy.83), calls=%async_computation.2 | async-start | bytes 16384 | tf_op jit(solution)/shard_map/all_to_all | solution.py:130
  240.2 2.0 copy-start.1
  643.1 100.2 %all-to-all-start.1 = ((f32[16,1,65536]{2,1,0:T(1,128)}), f32[16,1,65536]{2,1,0:T(1,128)}, u32[]{:S(2)}, u32[]{:S(2)}) async-start(f32[16,1,65536]{2,1,0:T(1,128)} %copy.82), calls=%async_computation.1 | async-start | bytes 8388608 | tf_op jit(solution)/shard_map/all_to_all | solution.py:129
  655.2 98.9 %copy-start.3 = (f32[4,1,1,128,4,1,128]{6,5,4,3,2,1,0:T(1,128)S(1)}, f32[4,1,1,128,4,1,128]{6,5,4,3,2,1,0:T(1,128)}, u32[]{:S(2)}) copy-start(f32[4,1,1,128,4,1,128]{6,5,4,3,2,1,0:T(1,128)} %param.5) | copy-start | bytes 3145732
Sparse Core Ops, SparseCore 0:
  12.2 79.5 all-gather.4
Sparse Core Ops, SparseCore 1:
  108.5 84.8 all-gather.6
